TPU v7x, 32 devices: a whole 2x2x4 slice. The times are simulated.
32 devices in a mesh: dp: 8 (over z, x), tensor: 4 (over y, core).
Axes of the slice: x: 2, y: 2, z: 4, core: 2. Of those that a mesh axis runs over, the one named last changes fastest.
Arguments:
- hidden: bfloat16 [16384, 1024], P('dp'), may hold values from -6 to 6
- lengths: int32 [8], P('dp'), may hold values from 1365 to 2048, as said below
- norm_gain: float32 [1024], replicated, may hold values from 0.1 to 1.9
- z_weight: bfloat16 [1024, 2048], P(None, 'tensor'), may hold values from -0.1875 to 0.1875
- x_weight: bfloat16 [1024, 2048], P(None, 'tensor'), may hold values from -0.1875 to 0.1875
- bc_weight: bfloat16 [1024, 256], replicated, may hold values from -0.1875 to 0.1875
- dt_weight: bfloat16 [1024, 32], P(None, 'tensor'), may hold values from -0.1875 to 0.1875
- x_kernel: float32 [4, 2048], P(None, 'tensor'), may hold values from -3 to 3
- bc_kernel: float32 [4, 256], replicated, may hold values from -3 to 3
- x_offset: float32 [2048], P('tensor'), may hold values from -3 to 3
- bc_offset: float32 [256], replicated, may hold values from -3 to 3
- step_bias: float32 [32], P('tensor'), may hold values from -5 to -1
- decay_log: float32 [32], P('tensor'), may hold values from 0 to 2.5
- skip_gain: float32 [32], P('tensor'), may hold values from 0.5 to 1.5
- gate_gain: float32 [2048], P('tensor'), may hold values from 0.1 to 1.9
- out_weight: bfloat16 [2048, 1024], P('tensor'), may hold values from -0.125 to 0.125
- cotangent: bfloat16 [16384, 1024], P('dp'), may hold values from -6 to 6
Outputs:
- output: bfloat16 [16384, 1024], P('dp')
- grad_hidden: float32 [16384, 1024], P('dp')
- grad_norm_gain: float32 [1024], replicated
- grad_z_weight: float32 [1024, 2048], P(None, 'tensor')
- grad_x_weight: float32 [1024, 2048], P(None, 'tensor')
- grad_bc_weight: float32 [1024, 256], replicated
- grad_dt_weight: float32 [1024, 32], P(None, 'tensor')
- grad_x_kernel: float32 [4, 2048], P(None, 'tensor')
- grad_bc_kernel: float32 [4, 256], replicated
- grad_x_offset: float32 [2048], P('tensor')
- grad_bc_offset: float32 [256], replicated
- grad_step_bias: float32 [32], P('tensor')
- grad_decay_log: float32 [32], P('tensor')
- grad_skip_gain: float32 [32], P('tensor')
- grad_gate_gain: float32 [2048], P('tensor')
- grad_out_weight: float32 [2048, 1024], P('tensor')
Inputs may be any that keep to these rules, and one draw needn't show every extreme that they name: `lengths`: each slot's sequence length; some slot has exactly 2048 in every draw.
All inputs are finite; a program needn't handle non-finite values.
Results may differ from a plain program's by a relative error of at most 0.0096.
Values may be sent and summed in bfloat16 or wider, within the bound.
No kernel may reach another device: no remote copies, remote signals or barrier semaphores. Data moves between devices by JAX's collectives and lax.ppermute only.
A program may use at most 192 MiB of HBM per device.

v0:
```python
import jax
import jax.numpy as jnp
from jax import lax
from jax.sharding import PartitionSpec as P

CH = 256
DI = 2048


precise = lax.Precision.HIGHEST
epsilon = 1e-05


def causal_conv(signal, kernel, offset):
    taps = kernel.shape[0]
    length = signal.shape[0]
    padded = jnp.pad(signal, ((taps - 1, 0), (0, 0)))
    total = jnp.zeros_like(signal) + offset[None, :]
    for tap_index in range(taps):
        total = total + kernel[tap_index][None, :] * padded[tap_index : tap_index + length]
    return total


def conv_act(signal, kernel, offset):
    return jax.nn.silu(causal_conv(signal, kernel, offset))


def group_step(carry_state, block_in):
    values, log_rates, b_rows, c_rows = block_in
    block_len = log_rates.shape[1]
    causal_mask = lax.broadcasted_iota(
        jnp.int32, (block_len, block_len), 0
    ) >= lax.broadcasted_iota(jnp.int32, (block_len, block_len), 1)
    summed = jnp.cumsum(log_rates, axis=1)
    spread = summed[:, :, None] - summed[:, None, :]
    decays = jnp.exp(jnp.where(causal_mask[None], spread, -1e30))
    scores = jnp.dot(c_rows, b_rows.T, precision=precise, preferred_element_type=jnp.float32)
    within = jnp.einsum("hts,hsp->htp", scores[None] * decays, values, precision=precise)
    carried = (
        jnp.einsum("tn,hnp->htp", c_rows, carry_state, precision=precise)
        * jnp.exp(summed)[:, :, None]
    )
    remain = jnp.exp(summed[:, -1:] - summed)
    updated = carry_state * jnp.exp(summed[:, -1])[:, None, None] + jnp.einsum(
        "sn,hsp->hnp", b_rows, values * remain[:, :, None], precision=precise
    )
    return (updated, within + carried)


def mixer(conv_vals, state_vals, step_raw, step_bias, decay_log, skip_gain, live_mask):
    row_count, channels = conv_vals.shape
    head_count = step_raw.shape[1]
    head_size = channels // head_count
    state_size = state_vals.shape[1] // 2
    block_count = row_count // CH
    step_size = jax.nn.softplus(step_raw + step_bias[None, :]) * live_mask[:, None]
    log_rates = step_size * (-jnp.exp(decay_log))[None, :]
    heads_view = conv_vals.reshape(row_count, head_count, head_size)
    values = heads_view * step_size[:, :, None]
    values = values.reshape(block_count, CH, head_count, head_size).transpose(0, 2, 1, 3)
    log_rates = log_rates.reshape(block_count, CH, head_count).transpose(0, 2, 1)
    b_rows = state_vals[:, :state_size].reshape(block_count, CH, state_size)
    c_rows = state_vals[:, state_size:].reshape(block_count, CH, state_size)
    start_state = jnp.zeros((head_count, state_size, head_size), jnp.float32)
    unused, results = lax.scan(
        jax.checkpoint(group_step), start_state, (values, log_rates, b_rows, c_rows)
    )
    mixed = results.transpose(0, 2, 1, 3).reshape(row_count, head_count, head_size)
    mixed = mixed + skip_gain[None, :, None] * heads_view
    return mixed.reshape(row_count, channels)


def gram(left, right):
    return lax.dot_general(
        left, right, (((0,), (0,)), ((), ())), preferred_element_type=jnp.float32
    )


def back_proj(grad_rows, weight):
    return lax.dot_general(
        grad_rows, weight, (((1,), (1,)), ((), ())), preferred_element_type=jnp.float32
    )


def rounded(value):
    return lax.optimization_barrier(value.astype(jnp.bfloat16)).astype(jnp.float32)


def body(
    hidden,
    lengths,
    norm_gain,
    z_weight,
    x_weight,
    bc_weight,
    dt_weight,
    x_kernel,
    bc_kernel,
    x_offset,
    bc_offset,
    step_bias,
    decay_log,
    skip_gain,
    gate_gain,
    out_weight,
    cotangent,
):
    row_count, model_width = hidden.shape
    parts = lax.axis_size("tensor")
    share = row_count // parts
    start = lax.axis_index("tensor") * share
    inputs = hidden.astype(jnp.float32)
    grad_out = cotangent.astype(jnp.float32)
    live_mask = (lax.iota(jnp.int32, row_count) < lengths[0]).astype(jnp.float32)
    scale = lax.rsqrt(jnp.mean(inputs * inputs, axis=1, keepdims=True) + epsilon)
    normed = (inputs * scale * norm_gain[None, :]).astype(jnp.bfloat16)
    gate_pre = jnp.dot(normed, z_weight, preferred_element_type=jnp.float32)
    conv_in = jnp.dot(normed, x_weight, preferred_element_type=jnp.float32)
    state_in = jnp.dot(normed, bc_weight, preferred_element_type=jnp.float32)
    step_raw = jnp.dot(normed, dt_weight, preferred_element_type=jnp.float32)
    conv_out, conv_pull = jax.vjp(conv_act, conv_in, x_kernel, x_offset)
    state_out, state_pull = jax.vjp(conv_act, state_in, bc_kernel, bc_offset)
    conv_low = rounded(conv_out)
    state_low = rounded(state_out)

    def local_mixer(conv_vals, state_vals, raw_steps, bias_steps, decay_logs, skip_gains):
        return mixer(
            conv_vals, state_vals, raw_steps, bias_steps, decay_logs, skip_gains, live_mask
        )

    mixed_out, mixer_pull = jax.vjp(
        local_mixer, conv_low, state_low, step_raw, step_bias, decay_log, skip_gain
    )
    sigmoid_gate = jax.nn.sigmoid(gate_pre)
    silu_gate = gate_pre * sigmoid_gate
    gated = mixed_out * silu_gate
    squares = lax.psum(jnp.sum(gated * gated, axis=1), "tensor")
    inv_norm = lax.rsqrt(squares / DI + epsilon)[:, None]
    unit_rows = gated * inv_norm
    branch_in = (unit_rows * gate_gain[None, :] * live_mask[:, None]).astype(jnp.bfloat16)
    own_inputs = lax.dynamic_slice_in_dim(inputs, start, share, 0)
    own_scale = lax.dynamic_slice_in_dim(scale, start, share, 0)
    branch = lax.psum(jnp.dot(branch_in, out_weight, preferred_element_type=jnp.float32), "tensor")
    output = (inputs + branch).astype(jnp.bfloat16)
    grad_out_weight = gram(branch_in, cotangent)
    grad_branch = back_proj(cotangent, out_weight) * live_mask[:, None]
    grad_gate_gain = jnp.sum(grad_branch * unit_rows, axis=0)
    grad_unit = grad_branch * gate_gain[None, :]
    cross = lax.psum(jnp.sum(grad_unit * unit_rows, axis=1), "tensor")
    grad_gated = inv_norm * (grad_unit - unit_rows * (cross / DI)[:, None])
    grad_mixed = grad_gated * silu_gate
    grad_gate_pre = grad_gated * mixed_out * sigmoid_gate * (1.0 + gate_pre * (1.0 - sigmoid_gate))
    (
        grad_conv_low,
        grad_state_part,
        grad_step_raw,
        grad_step_bias,
        grad_decay_log,
        grad_skip_gain,
    ) = mixer_pull(grad_mixed)
    grad_state_low = lax.psum(grad_state_part, "tensor")
    grad_conv_in, grad_x_kernel, grad_x_offset = conv_pull(grad_conv_low)
    grad_state_in, grad_bc_kernel, grad_bc_offset = state_pull(grad_state_low)
    low_gate = grad_gate_pre.astype(jnp.bfloat16)
    low_conv = grad_conv_in.astype(jnp.bfloat16)
    low_step = grad_step_raw.astype(jnp.bfloat16)
    low_state = lax.dynamic_slice_in_dim(grad_state_in, start, share, 0).astype(jnp.bfloat16)
    own_normed = lax.dynamic_slice_in_dim(normed, start, share, 0)
    grad_z_weight = gram(normed, low_gate)
    grad_x_weight = gram(normed, low_conv)
    grad_dt_weight = gram(normed, low_step)
    grad_bc_weight = gram(own_normed, low_state)
    state_back = back_proj(low_state, bc_weight)
    grad_normed = (
        back_proj(low_gate, z_weight)
        + back_proj(low_conv, x_weight)
        + back_proj(low_step, dt_weight)
    )
    own_part = lax.dynamic_slice_in_dim(grad_normed, start, share, 0) + state_back
    grad_normed = lax.dynamic_update_slice_in_dim(grad_normed, own_part, start, 0)
    grad_normed = lax.psum(grad_normed, "tensor")
    weighted = grad_normed * norm_gain[None, :]
    row_dots = jnp.sum(weighted * inputs, axis=1, keepdims=True)
    grad_hidden = (
        grad_out + scale * weighted - inputs * scale * scale * scale * row_dots / model_width
    )
    own_grad = lax.dynamic_slice_in_dim(grad_normed, start, share, 0)
    grad_norm_gain = jnp.sum(own_grad * own_inputs * own_scale, axis=0)
    (
        grad_z_weight,
        grad_x_weight,
        grad_dt_weight,
        grad_out_weight,
        grad_x_kernel,
        grad_x_offset,
        grad_step_bias,
        grad_decay_log,
        grad_skip_gain,
        grad_gate_gain,
        grad_bc_kernel,
        grad_bc_offset,
    ) = lax.psum(
        (
            grad_z_weight,
            grad_x_weight,
            grad_dt_weight,
            grad_out_weight,
            grad_x_kernel,
            grad_x_offset,
            grad_step_bias,
            grad_decay_log,
            grad_skip_gain,
            grad_gate_gain,
            grad_bc_kernel,
            grad_bc_offset,
        ),
        "dp",
    )
    grad_bc_weight, grad_norm_gain = lax.psum((grad_bc_weight, grad_norm_gain), ("dp", "tensor"))
    return (
        output,
        grad_hidden,
        grad_norm_gain,
        grad_z_weight,
        grad_x_weight,
        grad_bc_weight,
        grad_dt_weight,
        grad_x_kernel,
        grad_bc_kernel,
        grad_x_offset,
        grad_bc_offset,
        grad_step_bias,
        grad_decay_log,
        grad_skip_gain,
        grad_gate_gain,
        grad_out_weight,
    )


def solution(mesh):
    placed = (
        P("dp", None),
        P("dp"),
        P(),
        P(None, "tensor"),
        P(None, "tensor"),
        P(),
        P(None, "tensor"),
        P(None, "tensor"),
        P(),
        P("tensor"),
        P(),
        P("tensor"),
        P("tensor"),
        P("tensor"),
        P("tensor"),
        P("tensor", None),
        P("dp", None),
    )
    return jax.shard_map(
        body,
        mesh=mesh,
        in_specs=placed,
        out_specs=(
            P("dp", None),
            P("dp", None),
            P(),
            P(None, "tensor"),
            P(None, "tensor"),
            P(),
            P(None, "tensor"),
            P(None, "tensor"),
            P(),
            P("tensor"),
            P(),
            P("tensor"),
            P("tensor"),
            P("tensor"),
            P("tensor"),
            P("tensor", None),
        ),
        check_vma=False,
    )
```

profile of v0, /device:TPU:0, one launch (start us, length us, event | category | flops | bytes accessed | tf_op | source)
XLA Modules:
  0.0 1183.7 jit_solution(3214508663125442144)
XLA Ops:
  41.5 111.8 %while.39 = (s32[]{:T(128)}, f32[8,128,64]{1,2,0:T(8,128)}, f32[8,8,256,64]{2,3,1,0:T(8,128)}, f32[8,8,128,64]{2,3,1,0:T(8,128)}, f32[8,8,256]{2,1,0:T(8,128)}, ...) while((s32[]{:T(128)}, f32[8,128,64]{1,2,0:T(8,128)}, ...), condition=%wide.region_4.5_spmd.clone, body=%wide.region_1.4_spmd.clone.sunk | while | flops 908396544 | bytes 5419819 | solution.py:65
  153.4 7.1 copy.92
  160.5 7.5 reshape.567
  168.1 10.3 multiply_reduce_fusion.13
  178.4 8.5 psum.133
  187.0 9.5 multiply_reduce_fusion.5
  202.3 11.1 multiply_reduce_fusion.6
  230.1 202.8 %while.40 = (s32[]{:T(128)}, f32[8,128,64]{1,2,0:T(8,128)S(1)}, f32[8,8,256,64]{2,3,1,0:T(8,128)}, f32[8,8,256]{2,1,0:T(8,128)}, f32[8,256,128]{2,1,0:T(8,128)},...) while((s32[]{:T(128)}, f32[8,128,64]{1,2,0:T(8,128)S(1)}, ...), condition=%wide.region_22.23_spmd.clone, body=%wide.region_10.22_spmd.clone.sunk | while | flops 2122338304 | bytes 16312063 | solution.py:65
  436.3 8.0 fusion.107
  444.2 7.0 copy.93
  451.2 7.6 reshape.568
  474.5 7.0 multiply_reduce_fusion.10
  481.5 6.6 broadcast_multiply_fusion
  488.1 8.1 fusion.85
  507.7 10.3 add_add_fusion
  518.0 6.1 multiply_reduce_fusion.17
  529.7 6.7 fusion.126
  549.7 6.6 convert_element_type.48
  559.5 38.5 %all-reduce.22 = (f32[1024,8]{0,1:T(8,128)}, f32[4,512]{1,0:T(4,128)}, f32[4,256]{1,0:T(4,128)}, f32[512]{0:T(512)}, f32[256]{0:T(256)}, /*index=5*/f32[8]{0:T(128)}, f32[8]{0:T(128)}, f32[8]{0:T(128)}, f32[512]{0:T(512)}) all-reduce(f32[1024,8]{0,1:T(8,128)S(1)} %fusion.101, ...), channel_id=1, replica_groups=mesh['dp'=8,'tensor'=4] {'dp'}, use_global_device_ids=true, to_apply=%region_32.33 | all-reduce | flops 12568 | bytes 100544 | tf_op jit(solution)/shard_map/psum | solution.py:202
  598.0 220.2 %all-reduce.36.cloned.1.call-done = (f32[2048,1024]{1,0:T(8,128)}, f32[2048,1024]{1,0:T(8,128)}) async-done(((f32[2048,1024]{1,0:T(8,128)}, f32[2048,1024]{1,0:T(8,128)}), (f32[2048,1024]{1,0:T(8,128)}, f32[2048,1024]{1,0:T(8,128)})) %all-reduce.36.cloned.1.call-update) | async-done | bytes 16777232 | tf_op jit(solution)/shard_map/psum | solution.py:143
  820.7 40.0 %psum.138 = f32[1024]{0:T(1024)} all-reduce(f32[1024]{0:T(1024)S(1)} %multiply_reduce_fusion.18), channel_id=1, replica_groups=mesh['dp'=8,'tensor'=4] {'dp','tensor'}, use_global_device_ids=true, to_apply=%region_28.29 | all-reduce | flops 1024 | bytes 8192 | tf_op jit(solution)/shard_map/psum | solution.py:219
  869.1 9.5 multiply_subtract_fusion
  878.6 76.4 %all-reduce.32.cloned.1.call-done = f32[1024,256]{1,0:T(8,128)} async-done(((f32[1024,256]{1,0:T(8,128)}), f32[1024,256]{1,0:T(8,128)}) %all-reduce.32.cloned.1.call-update) | async-done | bytes 1048592 | tf_op jit(solution)/shard_map/psum | solution.py:219
  955.0 214.6 %all-reduce.34.cloned.1.call-done = (f32[1024,512]{1,0:T(8,128)}, f32[1024,512]{1,0:T(8,128)}, f32[512,1024]{1,0:T(8,128)}) async-done(((f32[1024,512]{1,0:T(8,128)}, f32[1024,512]{1,0:T(8,128)}, f32[512,1024]{1,0:T(8,128)}), (f32[1024,512]{1,0:T(8,128)}, f32[1024,512]{1,0:T(8,128)}, f32[512,1024]{1,0:T(8,128)})) %all-reduce.34.cloned.1.call-update) | async-done | bytes 6291472 | tf_op jit(solution)/shard_map/psum | solution.py:202
  (588 shorter events, 439.5 us)
Async XLA Ops:
  7.2 160.9 %copy-start = (bf16[1024,512]{1,0:T(8,128)(2,1)S(1)}, bf16[1024,512]{1,0:T(8,128)(2,1)}, u32[]{:S(2)}) copy-start(bf16[1024,512]{1,0:T(8,128)(2,1)} %param.24) | copy-start | bytes 3145732
  7.2 510.8 %all-reduce.30.cloned.1.call-start = ((), (), s32[]{:S(2)}) async-start(), calls=%async_computation | async-start | bytes 4194304 | tf_op jit(solution)/shard_map/psum | solution.py:161
  160.5 7.5 copy-start.62
  168.1 18.8 %copy-start.34 = (f32[512]{0:T(512)S(1)}, f32[512]{0:T(512)}, u32[]{:S(2)}) copy-start(f32[512]{0:T(512)} %param.35) | copy-start | bytes 6148
  436.0 382.2 %all-reduce.36.cloned.1.call-start = ((), (), s32[]{:S(2)}) async-start(), calls=%async_computation.3 | async-start | bytes 33554432 | tf_op jit(solution)/shard_map/psum | solution.py:143
  451.2 7.6 copy-start.20
  474.5 7.0 copy-start.36
  474.5 7.0 copy-start.38
  474.5 7.0 copy-start.40
  488.1 8.1 copy-start.64
  518.0 6.2 copy-start.46
  518.0 6.2 copy-start.48
  529.4 425.6 %all-reduce.32.cloned.1.call-start = ((), (), s32[]{:S(2)}) async-start(), calls=%async_computation.1 | async-start | bytes 2097152 | tf_op jit(solution)/shard_map/psum | solution.py:219
  529.7 6.7 copy-start.8
  529.7 6.7 copy-start.16
  543.0 626.7 %all-reduce.34.cloned.1.call-start = ((), (), s32[]{:S(2)}) async-start(), calls=%async_computation.2 | async-start | bytes 12582912 | tf_op jit(solution)/shard_map/psum | solution.py:202
  549.7 6.6 copy-start.49
  549.7 6.8 copy-start.50
  549.7 6.8 copy-start.51
  549.7 6.8 copy-start.52
  549.7 6.9 copy-start.53
  549.7 6.9 copy-start.66
  556.6 304.1 %copy-start.33 = (f32[1024]{0:T(1024)S(1)}, f32[1024]{0:T(1024)}, u32[]{:S(2)}) copy-start(f32[1024]{0:T(1024)} %param.23) | copy-start | bytes 12292
  860.7 8.4 copy-start.5
  (47 other events, 180.7 us)
Sparse Core Ops, SparseCore 0:
  436.1 51.6 all-reduce.29
  529.5 288.6 all-reduce.35
  823.9 131.0 all-reduce.31
  960.3 209.3 all-reduce.33
where the time goes:
time: 1190 us; the launch traced here: 1180 us
  waiting for transfers between devices  511 us (43%)
  matrix products  275 us (23%)
  local copies, waits for them, and re-layouts  150 us (13%)
  other arithmetic  136 us (11%)
  blocking collectives  92.8 us (8%)
  between operations  15.7 us (1%)
    psum x1, waiting for transfers between devices, body(): lax.psum(jnp.dot(branch_in, out_weight, preferred_element_type=jnp.float3...  220 us
    psum x1, waiting for transfers between devices, body(): lax.psum((grad_z_weight, grad_x_weight, grad_dt_weight, grad_out_weight,...  215 us
    dot_general x24, matrix products, group_step(): jnp.einsum('hts,hsp->htp', scores[None] * decays, values, precision=precise)  89.6 us
    psum x1, waiting for transfers between devices, body(): lax.psum((grad_bc_weight, grad_norm_gain), ('dp', 'tensor'))  76.4 us
    psum x1, blocking collectives, body(): lax.psum((grad_bc_weight, grad_norm_gain), ('dp', 'tensor'))  40 us
    another operation x57, other arithmetic  38.8 us
    psum x1, blocking collectives, body(): lax.psum((grad_z_weight, grad_x_weight, grad_dt_weight, grad_out_weight,...  38.5 us
    dot_general x24, matrix products, group_step(): jnp.einsum('sn,hsp->hnp', b_rows, values * remain[:, :, None], precision=...  37.8 us
  transfers between devices with their start and end apart: 4, of which 3 were waited for; matrix products, arithmetic and copies ran while one was open for 11% of the time, Pallas kernels for 0%

commit v1 on v0

--- a/solution.py
+++ b/solution.py
@@ -25,49 +25,38 @@
     return jax.nn.silu(causal_conv(signal, kernel, offset))
 
 
-def group_step(carry_state, block_in):
-    values, log_rates, b_rows, c_rows = block_in
-    block_len = log_rates.shape[1]
-    causal_mask = lax.broadcasted_iota(
-        jnp.int32, (block_len, block_len), 0
-    ) >= lax.broadcasted_iota(jnp.int32, (block_len, block_len), 1)
-    summed = jnp.cumsum(log_rates, axis=1)
-    spread = summed[:, :, None] - summed[:, None, :]
-    decays = jnp.exp(jnp.where(causal_mask[None], spread, -1e30))
-    scores = jnp.dot(c_rows, b_rows.T, precision=precise, preferred_element_type=jnp.float32)
-    within = jnp.einsum("hts,hsp->htp", scores[None] * decays, values, precision=precise)
-    carried = (
-        jnp.einsum("tn,hnp->htp", c_rows, carry_state, precision=precise)
-        * jnp.exp(summed)[:, :, None]
-    )
-    remain = jnp.exp(summed[:, -1:] - summed)
-    updated = carry_state * jnp.exp(summed[:, -1])[:, None, None] + jnp.einsum(
-        "sn,hsp->hnp", b_rows, values * remain[:, :, None], precision=precise
-    )
-    return (updated, within + carried)
-
-
 def mixer(conv_vals, state_vals, step_raw, step_bias, decay_log, skip_gain, live_mask):
-    row_count, channels = conv_vals.shape
-    head_count = step_raw.shape[1]
-    head_size = channels // head_count
-    state_size = state_vals.shape[1] // 2
-    block_count = row_count // CH
+    R, channels = conv_vals.shape
+    h = step_raw.shape[1]
+    p = channels // h
+    n = state_vals.shape[1] // 2
+    nb = R // CH
     step_size = jax.nn.softplus(step_raw + step_bias[None, :]) * live_mask[:, None]
     log_rates = step_size * (-jnp.exp(decay_log))[None, :]
-    heads_view = conv_vals.reshape(row_count, head_count, head_size)
-    values = heads_view * step_size[:, :, None]
-    values = values.reshape(block_count, CH, head_count, head_size).transpose(0, 2, 1, 3)
-    log_rates = log_rates.reshape(block_count, CH, head_count).transpose(0, 2, 1)
-    b_rows = state_vals[:, :state_size].reshape(block_count, CH, state_size)
-    c_rows = state_vals[:, state_size:].reshape(block_count, CH, state_size)
-    start_state = jnp.zeros((head_count, state_size, head_size), jnp.float32)
-    unused, results = lax.scan(
-        jax.checkpoint(group_step), start_state, (values, log_rates, b_rows, c_rows)
-    )
-    mixed = results.transpose(0, 2, 1, 3).reshape(row_count, head_count, head_size)
-    mixed = mixed + skip_gain[None, :, None] * heads_view
-    return mixed.reshape(row_count, channels)
+    heads_view = conv_vals.reshape(R, h, p)
+    vals = (heads_view * step_size[:, :, None]).reshape(nb, CH, h, p)
+    lr = log_rates.reshape(nb, CH, h)
+    B = state_vals[:, :n].reshape(nb, CH, n)
+    C = state_vals[:, n:].reshape(nb, CH, n)
+    tri = (lax.broadcasted_iota(jnp.int32, (CH, CH), 0) >= lax.broadcasted_iota(jnp.int32, (CH, CH), 1))
+    summed = jnp.einsum('ts,bsh->bth', tri.astype(jnp.float32), lr, precision=precise)
+    spread = summed[:, :, None, :] - summed[:, None, :, :]
+    decays = jnp.exp(jnp.where(tri[None, :, :, None], spread, -1e30))
+    scores = jnp.einsum('btn,bsn->bts', C, B, precision=precise)
+    within = jnp.einsum('btsh,bshp->bthp', scores[:, :, :, None] * decays, vals, precision=precise)
+    totals = summed[:, -1, :]
+    remain = jnp.exp(totals[:, None, :] - summed)
+    chunk = jnp.einsum('bsn,bshp->bhnp', B, vals * remain[..., None], precision=precise)
+    tc = jnp.cumsum(totals, axis=0)
+    tcp = tc - totals
+    bi = lax.broadcasted_iota(jnp.int32, (nb, nb), 0)
+    bj = lax.broadcasted_iota(jnp.int32, (nb, nb), 1)
+    gap = tcp[:, None, :] - tc[None, :, :]
+    mprev = jnp.exp(jnp.where((bj < bi)[:, :, None], gap, -1e30))
+    start = jnp.einsum('bjh,jhnp->bhnp', mprev, chunk, precision=precise)
+    carried = jnp.einsum('btn,bhnp->bthp', C, start, precision=precise) * jnp.exp(summed)[..., None]
+    mixed = (within + carried).reshape(R, h, p) + skip_gain[None, :, None] * heads_view
+    return mixed.reshape(R, channels)
 
 
 def gram(left, right):

time: 1190 us -> 999 us (0.84)
  matrix products: 275 us -> 195 us
  local copies, waits for them, and re-layouts: 150 us -> 88.4 us
  other arithmetic: 136 us -> 87.8 us
    dot_general x104 -> x16, matrix products: 177 us -> 110 us  [the longest x3 61.6 us: mixer(): jnp.einsum('btsh,bshp->bthp', scores[:, :, :, None] * decays, vals, preci...]
    squeeze x32 -> x0, local copies, waits for them, and re-layouts: 30.4 us -> none  [mixer(): lax.scan(jax.checkpoint(group_step), start_state, (values, log_rates, b_r...]
    another operation x65 -> x3, other arithmetic: 38.9 us -> 8.95 us
    dynamic_slice x8 -> x0, local copies, waits for them, and re-layouts: 20.6 us -> none  [mixer(): lax.scan(jax.checkpoint(group_step), start_state, (values, log_rates, b_r...]
    while x8 -> x0, matrix products: 18.2 us -> none
    dynamic_update_slice x16 -> x0, other arithmetic: 18.1 us -> none  [mixer(): lax.scan(jax.checkpoint(group_step), start_state, (values, log_rates, b_r...]
    another operation x61 -> x3, local copies, waits for them, and re-layouts: 16.2 us -> 0.27 us  [the longest x2 0.19 us: mixer(): tc = jnp.cumsum(totals, axis=0)]
    reshape x13 -> x7, local copies, waits for them, and re-layouts: 32.9 us -> 45.2 us  [the longest x3 19.5 us: mixer(): vals = (heads_view * step_size[:, :, None]).reshape(nb, CH, h, p)]
  transfers between devices with their start and end apart: 4 -> 4, of which waited for: 3 -> 3; matrix products, arithmetic and copies ran while one was open for 11% -> 18% of each run, Pallas kernels for 0% -> 0%
where the time goes in v1:
time: 999 us; the launch traced here: 992 us
  waiting for transfers between devices  512 us (51%)
  matrix products  195 us (20%)
  blocking collectives  92.8 us (9%)
  local copies, waits for them, and re-layouts  88.4 us (9%)
  other arithmetic  87.8 us (9%)
  between operations  16.1 us (2%)
    psum x1, waiting for transfers between devices, body(): lax.psum(jnp.dot(branch_in, out_weight, preferred_element_type=jnp.float3...  220 us
    psum x1, waiting for transfers between devices, body(): lax.psum((grad_z_weight, grad_x_weight, grad_dt_weight, grad_out_weight,...  215 us
    psum x1, waiting for transfers between devices, body(): lax.psum((grad_bc_weight, grad_norm_gain), ('dp', 'tensor'))  76.6 us
    dot_general x3, matrix products, mixer(): jnp.einsum('btsh,bshp->bthp', scores[:, :, :, None] * decays, vals, preci...  61.6 us
    psum x1, blocking collectives, body(): lax.psum((grad_bc_weight, grad_norm_gain), ('dp', 'tensor'))  39.9 us
    psum x1, blocking collectives, body(): lax.psum((grad_z_weight, grad_x_weight, grad_dt_weight, grad_out_weight,...  38.6 us
    dot_general x5, matrix products, back_proj(): lax.dot_general(grad_rows, weight, (((1,), (1,)), ((), ())), preferred_el...  34.3 us
    unnamed x193, local copies, waits for them, and re-layouts  22.5 us
  transfers between devices with their start and end apart: 4, of which 3 were waited for; matrix products, arithmetic and copies ran while one was open for 18% of the time, Pallas kernels for 0%

profile of v1, /device:TPU:0, one launch (start us, length us, event | category | flops | bytes accessed | tf_op | source)
XLA Modules:
  0.0 991.9 jit_solution(8709993499033490495)
XLA Ops:
  25.9 7.0 copy.119
  55.6 20.8 %bitcast_add_fusion.1 = f32[8,256,8,64]{1,3,2,0:T(8,128)} fusion(f32[8,256,8,64]{1,3,2,0:T(8,128)S(1)} %bitcast.172, f32[8,256,8]{1,2,0:T(8,128)S(1)} %get-tuple-element.75, f32[8,256,8]{1,2,0:T(8,128)S(1)} %convolution_bitcast_fusion, f32[8,256,256]{2,1,0:T(8,128)S(1)} %fusion.160, pred[256,256]{1,0:T(8,128)(4,1)S(1)} %iota_compare_fusion, ...), kind=kOutput, calls=%fused_computation.36 | convolution fusion | flops 3236954112 | bytes 14942208 | tf_op jit(solution)/shard_map/jvp(btsh,bshp->bthp)/dot_general | solution.py:46
  83.3 7.5 reshape.285
  90.9 10.3 %multiply_reduce_fusion.12 = (f32[2048]{0:T(1024)S(1)}, f32[2048,512]{1,0:T(8,128)}, f32[2048,512]{1,0:T(8,128)}) fusion(f32[2048,512]{1,0:T(8,128)} %reshape.285, bf16[2048,512]{1,0:T(8,128)(2,1)S(1)} %get-tuple-element.57, f32[512]{0:T(512)S(1)} %mul.539, bf16[2048,1024]{1,0:T(8,128)(2,1)} %copy-done.1, bf16[1024,512]{1,0:T(8,128)(2,1)S(1)} %copy-done), kind=kOutput, calls=%fused_computation.50 | convolution fusion | flops 2157967360 | bytes 19933184 | tf_op jit(solution)/shard_map/dot_general | solution.py:106
  101.2 8.5 psum.133
  109.7 9.5 multiply_reduce_fusion.2
  125.1 11.1 %multiply_reduce_fusion.3 = (f32[512]{0:T(512)}, f32[2048,512]{1,0:T(8,128)}, bf16[2048,512]{1,0:T(8,128)(2,1)}) fusion(bf16[2048,512]{1,0:T(8,128)(2,1)S(1)} %get-tuple-element.57, f32[2048,512]{1,0:T(8,128)} %get-tuple-element.88, f32[2048]{0:T(1024)S(1)} %broadcast_multiply_fusion.9, f32[2048,512]{1,0:T(8,128)} %get-tuple-element.54, ...), kind=kLoop, calls=%fused_computation.38 | loop fusion | flops 24116736 | bytes 25196544 | tf_op jit(solution)/shard_map/transpose(jvp())/reduce_sum | solution.py:58
  145.9 24.5 %fusion.9 = (f32[8,256,8]{1,2,0:T(8,128)}, f32[8,256,8]{1,2,0:T(8,128)}, f32[8,256,256]{2,1,0:T(8,128)S(1)}) fusion(f32[8,256,8]{1,2,0:T(8,128)S(1)} %convolution_bitcast_fusion, f32[8,256,256]{2,1,0:T(8,128)S(1)} %copy-done.35, pred[256,256]{1,0:T(8,128)(4,1)S(1)} %copy-done.45, f32[8,256,8,64]{1,3,2,0:T(8,128)S(1)} %copy-done.5, ...), kind=kOutput, calls=%fused_computation.10 | convolution fusion | flops 3259465728 | bytes 12910592 | tf_op jit(solution)/shard_map/transpose(jvp(btsh,bshp->bthp))/dot_general | solution.py:46
  170.4 7.7 fusion.77
  197.9 7.3 multiply_reduce_fusion.8
  205.2 7.3 fusion.146
  217.5 8.5 fusion.145
  226.1 16.3 %bitcast_add_fusion = f32[8,256,8,64]{1,3,2,0:T(8,128)} fusion(f32[8,256,8,64]{1,3,2,0:T(8,128)S(1)} %copy-done.33, f32[8,256,8]{1,2,0:T(8,128)S(1)} %get-tuple-element.76, f32[8,256,8]{1,2,0:T(8,128)S(1)} %convolution_bitcast_fusion, f32[8,256,256]{2,1,0:T(8,128)S(1)} %copy-done.36, pred[256,256]{1,0:T(8,128)(4,1)S(1)} %copy-done.46, ...), kind=kOutput, calls=%fused_computation.35 | convolution fusion | flops 3235905536 | bytes 14876672 | tf_op jit(solution)/shard_map/transpose(jvp(btsh,bshp->bthp))/dot_general | solution.py:46
  242.4 7.0 copy.164
  249.3 7.5 reshape.286
  273.3 11.3 %multiply_reduce_fusion.7 = (f32[512]{0:T(512)}, f32[512]{0:T(512)}, f32[512]{0:T(512)}, f32[512]{0:T(512)}, f32[512]{0:T(512)}, /*index=5*/f32[2048,512]{1,0:T(8,128)S(1)}) fusion(f32[2048,512]{1,0:T(8,128)} %copy-done.20, f32[2048,512]{1,0:T(8,128)} %get-tuple-element.58, f32[2048,512]{1,0:T(8,128)S(1)} %copy-done.19, f32[2048,512]{1,0:T(8,128)} %copy.135, ...), kind=kLoop, calls=%fused_computation.42 | loop fusion | flops 22017536 | bytes 25178112 | tf_op jit(solution)/shard_map/transpose(jvp())/reduce_sum | solution.py:20
  291.2 8.1 fusion.22
  315.8 10.3 %add_add_fusion = f32[2048,1024]{1,0:T(8,128)} fusion(f32[2048,1024]{1,0:T(8,128)} %fusion.162, f32[2048,1024]{1,0:T(8,128)} %fusion.163, bf16[1024,8]{0,1:T(8,128)(2,1)} %param.23, bf16[2048,8]{0,1:T(8,128)(2,1)S(1)} %get-tuple-element.50), kind=kOutput, calls=%fused_computation.13 | convolution fusion | flops 37748736 | bytes 25214976 | tf_op jit(solution)/shard_map/dot_general | solution.py:69
  367.5 38.6 %all-reduce.21 = (f32[1024,8]{0,1:T(8,128)}, f32[4,512]{1,0:T(4,128)}, f32[4,256]{1,0:T(4,128)}, f32[512]{0:T(512)}, f32[256]{0:T(256)}, /*index=5*/f32[8]{0:T(128)}, f32[8]{0:T(128)}, f32[8]{0:T(128)}, f32[512]{0:T(512)}) all-reduce(f32[1024,8]{0,1:T(8,128)S(1)} %fusion.124, ...), channel_id=1, replica_groups=mesh['dp'=8,'tensor'=4] {'dp'}, use_global_device_ids=true, to_apply=%region_25.26 | all-reduce | flops 12568 | bytes 100544 | tf_op jit(solution)/shard_map/psum | solution.py:191
  406.1 220.3 %all-reduce.35.cloned.1.call-done = (f32[2048,1024]{1,0:T(8,128)}, f32[2048,1024]{1,0:T(8,128)}) async-done(((f32[2048,1024]{1,0:T(8,128)}, f32[2048,1024]{1,0:T(8,128)}), (f32[2048,1024]{1,0:T(8,128)}, f32[2048,1024]{1,0:T(8,128)})) %all-reduce.35.cloned.1.call-update) | async-done | bytes 16777232 | tf_op jit(solution)/shard_map/psum | solution.py:132
  628.9 39.9 %psum.138 = f32[1024]{0:T(1024)} all-reduce(f32[1024]{0:T(1024)S(1)} %multiply_reduce_fusion.17), channel_id=1, replica_groups=mesh['dp'=8,'tensor'=4] {'dp','tensor'}, use_global_device_ids=true, to_apply=%region_21.22 | all-reduce | flops 1024 | bytes 8192 | tf_op jit(solution)/shard_map/psum | solution.py:208
  677.1 9.5 multiply_subtract_fusion
  686.6 76.6 %all-reduce.31.cloned.1.call-done = f32[1024,256]{1,0:T(8,128)} async-done(((f32[1024,256]{1,0:T(8,128)}), f32[1024,256]{1,0:T(8,128)}) %all-reduce.31.cloned.1.call-update) | async-done | bytes 1048592 | tf_op jit(solution)/shard_map/psum | solution.py:208
  763.2 214.6 %all-reduce.33.cloned.1.call-done = (f32[1024,512]{1,0:T(8,128)}, f32[1024,512]{1,0:T(8,128)}, f32[512,1024]{1,0:T(8,128)}) async-done(((f32[1024,512]{1,0:T(8,128)}, f32[1024,512]{1,0:T(8,128)}, f32[512,1024]{1,0:T(8,128)}), (f32[1024,512]{1,0:T(8,128)}, f32[1024,512]{1,0:T(8,128)}, f32[512,1024]{1,0:T(8,128)})) %all-reduce.33.cloned.1.call-update) | async-done | bytes 6291472 | tf_op jit(solution)/shard_map/psum | solution.py:191
  (279 shorter events, 186.0 us)
Async XLA Ops:
  7.2 83.8 %copy-start = (bf16[1024,512]{1,0:T(8,128)(2,1)S(1)}, bf16[1024,512]{1,0:T(8,128)(2,1)}, u32[]{:S(2)}) copy-start(bf16[1024,512]{1,0:T(8,128)(2,1)} %param.20) | copy-start | bytes 3145732
  7.2 318.9 %all-reduce.29.cloned.1.call-start = ((), (), s32[]{:S(2)}) async-start(), calls=%async_computation | async-start | bytes 4194304 | tf_op jit(solution)/shard_map/psum | solution.py:150
  7.3 39.3 %copy-start.64 = (pred[8,8]{1,0:T(8,128)(4,1)}, pred[8,8]{1,0:T(8,128)(4,1)S(1)}, u32[]{:S(2)}) copy-start(pred[8,8]{1,0:T(8,128)(4,1)S(1)} %iota_compare_fusion.4) | copy-start | bytes 196
  7.3 46.0 %copy-start.44 = (pred[256,256]{1,0:T(8,128)(4,1)}, pred[256,256]{1,0:T(8,128)(4,1)S(1)}, u32[]{:S(2)}) copy-start(pred[256,256]{1,0:T(8,128)(4,1)S(1)} %iota_compare_fusion) | copy-start | bytes 196612
  90.9 34.1 %copy-start.52 = (f32[512]{0:T(512)}, f32[512]{0:T(512)S(1)}, u32[]{:S(2)}) copy-start(f32[512]{0:T(512)S(1)} %mul.539) | copy-start | bytes 6148
  90.9 18.8 %copy-start.50 = (f32[512]{0:T(512)S(1)}, f32[512]{0:T(512)}, u32[]{:S(2)}) copy-start(f32[512]{0:T(512)} %param.31) | copy-start | bytes 6148
  145.8 32.3 %copy-start.6 = (f32[64,8,8,256]{3,2,1,0:T(8,128)}, f32[64,8,8,256]{3,2,1,0:T(8,128)S(1)}, u32[]{:S(2)}) copy-start(f32[64,8,8,256]{3,2,1,0:T(8,128)S(1)} %copy.172) | copy-start | bytes 12582916
  145.9 24.5 %copy-start.15 = (f32[8,8,128,64]{2,0,3,1:T(8,128)S(1)}, f32[8,8,128,64]{2,0,3,1:T(8,128)}, u32[]{:S(2)}) copy-start(f32[8,8,128,64]{2,0,3,1:T(8,128)} %copy-done.14) | copy-start | bytes 6291460
  197.5 428.9 %all-reduce.35.cloned.1.call-start = ((), (), s32[]{:S(2)}) async-start(), calls=%async_computation.3 | async-start | bytes 33554432 | tf_op jit(solution)/shard_map/psum | solution.py:132
  197.9 14.6 %copy-start.24 = (f32[8,256,512]{1,2,0:S(1)}, f32[8,256,512]{1,2,0}, u32[]{:S(2)}) copy-start(f32[8,256,512]{1,2,0} %copy-done.23) | copy-start | bytes 12582916
  217.5 8.5 copy-start.8
  217.5 8.5 copy-start.33
  217.5 8.5 copy-start.36
  217.5 8.5 copy-start.46
  259.3 12.8 %copy-start.53 = (f32[512]{0:T(512)S(1)}, f32[512]{0:T(512)}, u32[]{:S(2)}) copy-start(f32[512]{0:T(512)} %copy-done.52) | copy-start | bytes 6148
  273.2 11.3 %copy-start.55 = (f32[1,512]{1,0:T(1,128)S(1)}, f32[1,512]{1,0:T(1,128)}, u32[]{:S(2)}) copy-start(f32[1,512]{1,0:T(1,128)} %copy-done.54) | copy-start | bytes 6148
  273.2 11.3 %copy-start.57 = (f32[1,512]{1,0:T(1,128)S(1)}, f32[1,512]{1,0:T(1,128)}, u32[]{:S(2)}) copy-start(f32[1,512]{1,0:T(1,128)} %copy-done.56) | copy-start | bytes 6148
  273.2 11.3 %copy-start.59 = (f32[1,512]{1,0:T(1,128)S(1)}, f32[1,512]{1,0:T(1,128)}, u32[]{:S(2)}) copy-start(f32[1,512]{1,0:T(1,128)} %copy-done.58) | copy-start | bytes 6148
  273.2 11.3 %copy-start.61 = (f32[1,512]{1,0:T(1,128)S(1)}, f32[1,512]{1,0:T(1,128)}, u32[]{:S(2)}) copy-start(f32[1,512]{1,0:T(1,128)} %copy-done.60) | copy-start | bytes 6148
  291.2 8.1 copy-start.91
  337.5 425.7 %all-reduce.31.cloned.1.call-start = ((), (), s32[]{:S(2)}) async-start(), calls=%async_computation.1 | async-start | bytes 2097152 | tf_op jit(solution)/shard_map/psum | solution.py:208
  350.9 627.0 %all-reduce.33.cloned.1.call-start = ((), (), s32[]{:S(2)}) async-start(), calls=%async_computation.2 | async-start | bytes 12582912 | tf_op jit(solution)/shard_map/psum | solution.py:191
  364.6 304.1 %copy-start.49 = (f32[1024]{0:T(1024)S(1)}, f32[1024]{0:T(1024)}, u32[]{:S(2)}) copy-start(f32[1024]{0:T(1024)} %param.19) | copy-start | bytes 12292
  668.7 8.4 copy-start.9
  (74 other events, 342.2 us)
Sparse Core Ops, SparseCore 0:
  197.6 51.7 all-reduce.28
  337.7 288.6 all-reduce.34
  632.1 131.0 all-reduce.30
  768.5 209.3 all-reduce.32
